TPU v7x, 512 devices: a whole 4x4x16 slice. The times are simulated.
512 devices in a mesh: expert: 64 (over x, z_lo, core), shard: 8 (over z_hi, y).
Axes of the slice: x: 4, y: 4, z: 16 (z_hi: 2, z_lo: 8; z = z_hi * 8 + z_lo), core: 2. Of those that a mesh axis runs over, the one named last changes fastest.
Arguments:
- tokens: bfloat16 [2560, 4096], P('expert'), may hold values from -6 to 6
- expert_ids: int32 [2560, 8], P('expert'), may hold values from 0 to 63, all different within a row; in each aligned block of 40 rows (0 to 39, 40 to 79, ...) at most 10 rows name the same one
- route_weights: float32 [2560, 8], P('expert'), may hold values from 0.05 to 0.5
- partner: int32 [64], replicated, may hold values from 0 to 63, as said below
- gate_up: bfloat16 [64, 2, 768, 4096], P('expert', None, 'shard'), may hold values from -0.09375 to 0.09375
- down_weight: bfloat16 [64, 768, 4096], P('expert', None, 'shard'), may hold values from -0.21875 to 0.21875
- down_grad: bfloat16 [64, 128, 4096], P('expert', None, 'shard'), may hold values from -6 to 6
- moment_one: float32 [64, 128, 4096], P('expert', None, 'shard'), may hold values from -6 to 6
- moment_two: float32 [64, 128, 4096], P('expert', None, 'shard'), may hold values from 0.3 to 3
Outputs:
- combined: bfloat16 [2560, 4096], P('expert', 'shard')
- trained_rows: bfloat16 [64, 128, 4096], P('expert', None, 'shard')
- first_moment: float32 [64, 128, 4096], P('expert', None, 'shard')
- second_moment: float32 [64, 128, 4096], P('expert', None, 'shard')
Inputs may be any that keep to these rules, and one draw needn't show every extreme that they name: `expert_ids`: each row names 8 different experts. In each aligned block of 40 rows (the rows held by one index of expert) no expert is named by more than 10 rows, a bound that some block reaches. partner[partner[p]] = p and partner[p] != p for every p: the list splits all 64 indices into pairs.
All inputs are finite; a program needn't handle non-finite values.
Results may differ from a plain program's by a relative error of at most 0.0058.
Values may be sent and summed in bfloat16 or wider, within the bound.
No kernel may reach another device: no remote copies, remote signals or barrier semaphores. Data moves between devices by JAX's collectives and lax.ppermute only.
A program may use at most 64 MiB of HBM per device.

v0:
```python
import jax
import jax.numpy as jnp
from jax import lax
from jax.sharding import Mesh, PartitionSpec as P

STEP = 100


learn_rate = 0.01
beta_one = 0.9
beta_two = 0.999
epsilon = 1e-08
decay_rate = 0.1


def adamw(weight, gradient, first, second):
    grad_wide = gradient.astype(jnp.float32)
    first_new = beta_one * first + (1.0 - beta_one) * grad_wide
    second_new = beta_two * second + (1.0 - beta_two) * grad_wide * grad_wide
    first_hat = first_new / (1.0 - beta_one**STEP)
    second_hat = second_new / (1.0 - beta_two**STEP)
    weight_wide = weight.astype(jnp.float32)
    updated = weight_wide - learn_rate * (
        first_hat / (jnp.sqrt(second_hat) + epsilon) + decay_rate * weight_wide
    )
    return (updated.astype(jnp.bfloat16), first_new, second_new)


def shards(
    tokens,
    expert_ids,
    route_weights,
    partner,
    gate_up,
    down_weight,
    down_grad,
    moment_one,
    moment_two,
):
    groups = lax.axis_size("expert")
    quarters = lax.axis_size("y")
    token_count = tokens.shape[0]
    model_width = tokens.shape[1]
    part_width = down_weight.shape[2]
    trained = down_grad.shape[1]
    capacity = 2 * token_count * expert_ids.shape[1] // groups
    quarter = model_width // quarters
    new_rows, first_new, second_new = adamw(
        down_weight[:, :trained], down_grad, moment_one, moment_two
    )
    down_new = jnp.concatenate([new_rows, down_weight[:, trained:]], axis=1)
    pieces = (
        new_rows.reshape(groups, -1),
        first_new.astype(jnp.bfloat16).reshape(groups, -1),
        second_new.astype(jnp.bfloat16).reshape(groups, -1),
    )
    piece_width = sum(p.shape[1] for p in pieces)
    experts = jnp.arange(groups, dtype=jnp.int32)
    picked = (expert_ids[:, :, None] == experts[None, None, :]).astype(jnp.int32)
    running = jnp.cumsum(picked.reshape(-1, groups), axis=0).reshape(picked.shape)
    slot_index = jnp.sum((running - 1) * picked, axis=2)
    position = expert_ids * capacity + slot_index
    positions = jnp.arange(groups * capacity, dtype=jnp.int32)
    matches = position[None, :, :] == positions[:, None, None]
    dispatch = jnp.sum(matches.astype(jnp.int32), axis=2).astype(jnp.bfloat16)
    weighting = jnp.sum(jnp.where(matches, route_weights[None, :, :], 0.0), axis=2)
    own_quarter = lax.dynamic_slice_in_dim(tokens, lax.axis_index("y") * quarter, quarter, axis=1)
    outgoing = jnp.dot(dispatch, own_quarter, preferred_element_type=jnp.float32).astype(jnp.bfloat16)
    outgoing = jnp.concatenate([outgoing.reshape(groups, capacity * quarter)] + list(pieces), axis=1)
    received = lax.all_to_all(outgoing, "expert", split_axis=0, concat_axis=0, tiled=True)
    spread = received[:, capacity * quarter :]
    received = received[:, : capacity * quarter].reshape(groups * capacity, quarter)
    token_rows = lax.all_gather(received, "y", axis=0, tiled=False)
    joined = gate_up.reshape(-1, model_width)
    hidden_count = joined.shape[0] // 2
    projected = sum(
        lax.dot_general(
            joined[:, q * quarter : (q + 1) * quarter],
            token_rows[q],
            (((1,), (1,)), ((), ())),
            preferred_element_type=jnp.float32,
        )
        for q in range(quarters)
    )
    hidden = (jax.nn.silu(projected[:hidden_count]) * projected[hidden_count:]).astype(jnp.bfloat16)
    shard_count = lax.axis_size(("zh", "y"))
    copies = jnp.broadcast_to(hidden.reshape(1, -1), (shard_count, hidden.size))
    every_hidden = lax.all_to_all(copies, ("zh", "y"), split_axis=0, concat_axis=0, tiled=True)
    every_hidden = every_hidden.reshape(shard_count * hidden_count, -1)
    down_rows = down_new.reshape(-1, part_width)
    summed = lax.dot_general(
        every_hidden, down_rows, (((0,), (0,)), ((), ())), preferred_element_type=jnp.float32
    )
    results = summed.astype(jnp.bfloat16).reshape(groups, capacity * part_width)
    results = jnp.concatenate([results, jnp.take(spread, partner, axis=0)], axis=1)
    returned = lax.all_to_all(results, "expert", split_axis=0, concat_axis=0, tiled=True)
    back = returned[:, capacity * part_width :]
    returned = returned[:, : capacity * part_width]
    widths = [p.shape[1] for p in pieces]
    rows_out = back[:, : widths[0]].reshape(new_rows.shape)
    first_out = back[:, widths[0] : widths[0] + widths[1]].astype(jnp.float32).reshape(first_new.shape)
    second_out = back[:, widths[0] + widths[1] :].astype(jnp.float32).reshape(second_new.shape)
    returned_wide = returned.reshape(-1, part_width).astype(jnp.float32)
    combined = jnp.dot(
        weighting.T,
        returned_wide,
        precision=lax.Precision.HIGHEST,
        preferred_element_type=jnp.float32,
    ).astype(jnp.bfloat16)
    return (combined, rows_out, first_out, second_out)


def solution(mesh):
    shard_size = mesh.shape["shard"]
    quarters = 4 if shard_size % 4 == 0 else shard_size
    devices = mesh.devices.reshape(mesh.shape["expert"], shard_size // quarters, quarters)
    split_mesh = Mesh(devices, ("expert", "zh", "y"))
    sh = ("zh", "y")
    return jax.shard_map(
        shards,
        mesh=split_mesh,
        in_specs=(
            P("expert", None),
            P("expert", None),
            P("expert", None),
            P(),
            P("expert", None, sh, None),
            P("expert", None, sh),
            P("expert", None, sh),
            P("expert", None, sh),
            P("expert", None, sh),
        ),
        out_specs=(
            P("expert", sh),
            P("expert", None, sh),
            P("expert", None, sh),
            P("expert", None, sh),
        ),
        check_vma=False,
    )
```

profile of v0, /device:TPU:1, one launch (start us, length us, event | category | flops | bytes accessed | tf_op | source)
XLA Modules:
  0.0 359.1 jit_solution(18379436721601737755)
XLA Ops:
  7.2 0.8 copy.32
  8.2 0.9 reduce-window.6
  9.6 1.4 fusion.16
  11.0 0.7 reshape.94
  11.7 0.7 reshape.93
  12.4 0.7 reshape.92
  13.4 0.5 convolution_convert_fusion
  13.9 1.9 reshape.91
  15.8 1.1 maximum_bitcast_fusion
  17.0 0.5 broadcast.50
  17.5 2.6 reduce.4
  20.1 5.1 %reshape.123 = bf16[64,2,6656]{2,1,0:T(2,128)(2,1)} reshape(bf16[64,13312]{1,0:T(8,128)(2,1)} %reduce.4) | data formatting | bytes 3407872
  25.2 96.1 %all_to_all.30 = bf16[64,2,6656]{2,1,0:T(2,128)(2,1)S(1)} all-to-all(bf16[64,2,6656]{2,1,0:T(2,128)(2,1)} %reshape.123), channel_id=1, replica_groups=mesh['expert'=64,'zh'=2,'y'=4] {'expert'}, dimensions={0} | all-to-all | bytes 3407872 | tf_op jit(solution)/shard_map/all_to_all | solution.py:70
  121.3 3.9 %reshape.124 = bf16[64,1,13312]{2,1,0:T(2,128)(2,1)} reshape(bf16[64,2,6656]{2,1,0:T(2,128)(2,1)S(1)} %all_to_all.30) | data formatting | bytes 3407872
  125.2 2.5 copy.47
  127.7 1.3 copy-done.1
  129.0 2.8 all_gather_reshape.3
  131.9 61.2 %all-gather.2.cloned.1.call-done = bf16[4,640,1024]{2,1,0:T(8,128)(2,1)} async-done(((bf16[1,640,1024]{2,1,0:T(8,128)(2,1)}), bf16[4,640,1024]{2,1,0:T(8,128)(2,1)}) %all-gather.2.cloned.1.call-update) | async-done | bytes 5242896 | tf_op jit(solution)/shard_map/all_gather | solution.py:73
  193.0 2.1 fusion.1
  195.1 1.9 fusion.2
  197.0 0.6 fusion.5
  197.6 0.6 fusion.7
  198.4 1.0 broadcast_in_dim.39
  199.5 6.6 %reduce.5 = bf16[8,61440]{1,0:T(8,128)(2,1)S(1)} reduce(bf16[8,1,61440]{2,1,0:T(2,128)(2,1)S(1)} %broadcast_in_dim.39, bf16[]{:T(256)} %broadcast.50), dimensions={1}, to_apply=%broadcast_in_dim.39.reduce_sub_computation | reduce | bytes 1966082 | tf_op jit(solution)/shard_map/broadcast_in_dim | solution.py:87
  206.1 1.8 reshape.125
  207.9 13.7 %all-to-all-start.1 = ((bf16[8,2,30720]{2,1,0:T(2,128)(2,1)}), bf16[8,2,30720]{2,1,0:T(2,128)(2,1)S(1)}, u32[]{:S(2)}, u32[]{:S(2)}) async-start(bf16[8,2,30720]{2,1,0:T(2,128)(2,1)} %reshape.125), calls=%async_computation.1 | async-start | bytes 1966080 | tf_op jit(solution)/shard_map/all_to_all | solution.py:88
  221.6 1.0 slice.103
  222.6 0.8 gather_fusion
  223.4 0.9 broadcast_select_fusion
  224.3 31.4 %all-to-all-done.1 = bf16[8,2,30720]{2,1,0:T(2,128)(2,1)S(1)} async-done(((bf16[8,2,30720]{2,1,0:T(2,128)(2,1)}), bf16[8,2,30720]{2,1,0:T(2,128)(2,1)S(1)}, u32[]{:S(2)}, u32[]{:S(2)}) %all-to-all-start.1) | async-done | bytes 983072 | tf_op jit(solution)/shard_map/all_to_all | solution.py:88
  255.7 1.0 reshape.126
  256.7 6.0 %reduce.2 = bf16[8,61440]{1,0:T(8,128)(2,1)S(1)} reduce(bf16[8,1,61440]{2,1,0:T(2,128)(2,1)S(1)} %reshape.126, bf16[]{:T(256)} %constant.70), dimensions={1}, to_apply=%all_to_all.23.reduce_sub_computation | reduce | bytes 1966082 | tf_op jit(solution)/shard_map/all_to_all | solution.py:88
  262.7 0.4 reshape.96
  263.1 0.6 slice-done
  263.8 0.7 convolution_convert_fusion.1
  264.5 0.8 reshape.98
  265.3 1.4 reduce.6
  266.8 1.6 reshape.127
  268.4 26.2 %all-to-all-start.2 = ((bf16[64,2,4096]{2,1,0:T(2,128)(2,1)}), bf16[64,2,4096]{2,1,0:T(2,128)(2,1)S(1)}, u32[]{:S(2)}, u32[]{:S(2)}) async-start(bf16[64,2,4096]{2,1,0:T(2,128)(2,1)} %reshape.127), calls=%async_computation.2 | async-start | bytes 2097152 | tf_op jit(solution)/shard_map/all_to_all | solution.py:96
  294.7 1.0 select_reduce_fusion
  295.7 50.2 %all-to-all-done.2 = bf16[64,2,4096]{2,1,0:T(2,128)(2,1)S(1)} async-done(((bf16[64,2,4096]{2,1,0:T(2,128)(2,1)}), bf16[64,2,4096]{2,1,0:T(2,128)(2,1)S(1)}, u32[]{:S(2)}, u32[]{:S(2)}) %all-to-all-start.2) | async-done | bytes 1048608 | tf_op jit(solution)/shard_map/all_to_all | solution.py:96
  345.9 1.0 reshape.128
  347.0 1.1 copy.48
  348.2 0.8 reshape.99
  349.0 0.7 reshape.100
  349.7 0.7 reshape.107
  350.5 0.7 reshape.109
  351.2 1.0 convolution_convert_fusion.2
  (38 shorter events, 1.5 us)
Async XLA Ops:
  7.2 6.2 %copy-start = (bf16[40,4096]{1,0:T(8,128)(2,1)S(1)}, bf16[40,4096]{1,0:T(8,128)(2,1)}, u32[]{:S(2)}) copy-start(bf16[40,4096]{1,0:T(8,128)(2,1)} %param.9) | copy-start | bytes 983044
  7.2 185.9 %all-gather.2.cloned.1.call-start = ((), (), s32[]{:S(2)}) async-start(), calls=%async_computation.3 | async-start | bytes 6553600 | tf_op jit(solution)/shard_map/all_gather | solution.py:73
  127.7 1.3 copy-start.1
  129.0 64.0 %copy-start.5 = (bf16[1,2,96,4096]{3,2,1,0:T(8,128)(2,1)S(1)}, bf16[1,2,96,4096]{3,2,1,0:T(8,128)(2,1)}, u32[]{:S(2)}) copy-start(bf16[1,2,96,4096]{3,2,1,0:T(8,128)(2,1)} %param.13) | copy-start | bytes 4718596
  193.0 4.0 %copy-start.4 = (bf16[4,640,1024]{2,1,0:T(8,128)(2,1)S(1)}, bf16[4,640,1024]{2,1,0:T(8,128)(2,1)}, u32[]{:S(2)}) copy-start(bf16[4,640,1024]{2,1,0:T(8,128)(2,1)} %all-gather.2.cloned.1.call-done) | copy-start | bytes 15728644
  207.9 13.7 %copy-start.7 = (s32[64]{0:T(128)S(1)}, s32[64]{0:T(128)}, u32[]{:S(2)}) copy-start(s32[64]{0:T(128)} %param.12) | copy-start | bytes 772
  207.9 47.8 %all-to-all-start.1 = ((bf16[8,2,30720]{2,1,0:T(2,128)(2,1)}), bf16[8,2,30720]{2,1,0:T(2,128)(2,1)S(1)}, u32[]{:S(2)}, u32[]{:S(2)}) async-start(bf16[8,2,30720]{2,1,0:T(2,128)(2,1)} %reshape.125), calls=%async_computation.1 | async-start | bytes 1966080 | tf_op jit(solution)/shard_map/all_to_all | solution.py:88
  262.7 1.1 slice-start
  263.8 1.5 copy-start.2
  266.8 27.9 %copy-start.6 = (f32[40,8]{0,1:T(8,128)S(1)}, f32[40,8]{0,1:T(8,128)}, u32[]{:S(2)}) copy-start(f32[40,8]{0,1:T(8,128)} %param.11) | copy-start | bytes 3844
  268.4 77.5 %all-to-all-start.2 = ((bf16[64,2,4096]{2,1,0:T(2,128)(2,1)}), bf16[64,2,4096]{2,1,0:T(2,128)(2,1)S(1)}, u32[]{:S(2)}, u32[]{:S(2)}) async-start(bf16[64,2,4096]{2,1,0:T(2,128)(2,1)} %reshape.127), calls=%async_computation.2 | async-start | bytes 2097152 | tf_op jit(solution)/shard_map/all_to_all | solution.py:96
  348.2 3.0 copy-start.3
Sparse Core Ops, SparseCore 0:
  132.0 60.9 all-gather.1
where the time goes:
time: 360 us; the launch traced here: 359 us
  waiting for transfers between devices  143 us (40%)
  blocking collectives  96.1 us (27%)
  starting transfers between devices  40 us (11%)
  local copies, waits for them, and re-layouts  35.7 us (10%)
  other arithmetic  22.6 us (6%)
  between operations  14.4 us (4%)
  matrix products  7.43 us (2%)
    all_to_all x1, blocking collectives, shards(): lax.all_to_all(outgoing, 'expert', split_axis=0, concat_axis=0, tiled=True)  96.1 us
    all_gather x1, waiting for transfers between devices, shards(): token_rows = lax.all_gather(received, 'y', axis=0, tiled=False)  61.2 us
    all_to_all x1, waiting for transfers between devices, shards(): lax.all_to_all(results, 'expert', split_axis=0, concat_axis=0, tiled=True)  50.2 us
    all_to_all x1, waiting for transfers between devices, shards(): lax.all_to_all(copies, ('zh', 'y'), split_axis=0, concat_axis=0, tiled=True)  31.4 us
    all_to_all x1, starting transfers between devices, shards(): lax.all_to_all(results, 'expert', split_axis=0, concat_axis=0, tiled=True)  26.2 us
    unnamed x26, local copies, waits for them, and re-layouts  20.2 us
    all_to_all x1, starting transfers between devices, shards(): lax.all_to_all(copies, ('zh', 'y'), split_axis=0, concat_axis=0, tiled=True)  13.7 us
  transfers between devices with their start and end apart: 3, of which 3 were waited for; matrix products, arithmetic and copies ran while one was open for 1% of the time, Pallas kernels for 0%

commit v1 on v0

--- a/solution.py
+++ b/solution.py
@@ -67,21 +67,18 @@
     own_quarter = lax.dynamic_slice_in_dim(tokens, lax.axis_index("y") * quarter, quarter, axis=1)
     outgoing = jnp.dot(dispatch, own_quarter, preferred_element_type=jnp.float32).astype(jnp.bfloat16)
     outgoing = jnp.concatenate([outgoing.reshape(groups, capacity * quarter)] + list(pieces), axis=1)
+    joined = gate_up.reshape(-1, quarters, quarter)
+    hidden_count = joined.shape[0] // 2
+    by_quarter = jnp.moveaxis(joined, 1, 0)
+    quarter_weights = lax.all_to_all(by_quarter, "y", split_axis=0, concat_axis=0, tiled=True)
+    quarter_weights, outgoing = lax.optimization_barrier((quarter_weights, outgoing))
     received = lax.all_to_all(outgoing, "expert", split_axis=0, concat_axis=0, tiled=True)
     spread = received[:, capacity * quarter :]
     received = received[:, : capacity * quarter].reshape(groups * capacity, quarter)
-    token_rows = lax.all_gather(received, "y", axis=0, tiled=False)
-    joined = gate_up.reshape(-1, model_width)
-    hidden_count = joined.shape[0] // 2
-    projected = sum(
-        lax.dot_general(
-            joined[:, q * quarter : (q + 1) * quarter],
-            token_rows[q],
-            (((1,), (1,)), ((), ())),
-            preferred_element_type=jnp.float32,
-        )
-        for q in range(quarters)
+    partial = lax.dot_general(
+        quarter_weights, received, (((2,), (1,)), ((), ())), preferred_element_type=jnp.float32
     )
+    projected = lax.psum_scatter(partial, "y", scatter_dimension=0, tiled=False)
     hidden = (jax.nn.silu(projected[:hidden_count]) * projected[hidden_count:]).astype(jnp.bfloat16)
     shard_count = lax.axis_size(("zh", "y"))
     copies = jnp.broadcast_to(hidden.reshape(1, -1), (shard_count, hidden.size))

time: 360 us -> 350 us (0.972)
  waiting for transfers between devices: 143 us -> 118 us
  blocking collectives: 96.1 us -> 102 us
  local copies, waits for them, and re-layouts: 35.7 us -> 40.8 us
  starting transfers between devices: 40 us -> 44.2 us
    all_gather x1 -> x0, waiting for transfers between devices: 61.2 us -> none  [shards(): token_rows = lax.all_gather(received, 'y', axis=0, tiled=False)]
    reduce_scatter x0 -> x1, waiting for transfers between devices: none -> 30.9 us  [shards(): projected = lax.psum_scatter(partial, 'y', scatter_dimension=0, tiled=False)]
    reshape x0 -> x3, local copies, waits for them, and re-layouts: none -> 6.52 us  [the longest x2 4.55 us: shards(): joined = gate_up.reshape(-1, quarters, quarter)]
    all_to_all x1, blocking collectives: 96.1 us -> 102 us  [shards(): lax.all_to_all(outgoing, 'expert', split_axis=0, concat_axis=0, tiled=True)]
    all_to_all x0 -> x1, waiting for transfers between devices: none -> 5.73 us  [shards(): lax.all_to_all(by_quarter, 'y', split_axis=0, concat_axis=0, tiled=True)]
    all_to_all x0 -> x1, starting transfers between devices: none -> 5.13 us  [shards(): lax.all_to_all(by_quarter, 'y', split_axis=0, concat_axis=0, tiled=True)]
    unnamed x26 -> x28, local copies, waits for them, and re-layouts: 20.2 us -> 19.4 us
  transfers between devices with their start and end apart: 3 -> 4, of which waited for: 3 -> 4; matrix products, arithmetic and copies ran while one was open for 1% -> 4% of each run, Pallas kernels for 0% -> 0%
where the time goes in v1:
time: 350 us; the launch traced here: 349 us
  waiting for transfers between devices  118 us (34%)
  blocking collectives  102 us (29%)
  starting transfers between devices  44.2 us (13%)
  local copies, waits for them, and re-layouts  40.8 us (12%)
  other arithmetic  22.5 us (6%)
  between operations  14.4 us (4%)
  matrix products  7.2 us (2%)
    all_to_all x1, blocking collectives, shards(): lax.all_to_all(outgoing, 'expert', split_axis=0, concat_axis=0, tiled=True)  102 us
    all_to_all x1, waiting for transfers between devices, shards(): lax.all_to_all(results, 'expert', split_axis=0, concat_axis=0, tiled=True)  50.2 us
    all_to_all x1, waiting for transfers between devices, shards(): lax.all_to_all(copies, ('zh', 'y'), split_axis=0, concat_axis=0, tiled=True)  31.5 us
    reduce_scatter x1, waiting for transfers between devices, shards(): projected = lax.psum_scatter(partial, 'y', scatter_dimension=0, tiled=False)  30.9 us
    all_to_all x1, starting transfers between devices, shards(): lax.all_to_all(results, 'expert', split_axis=0, concat_axis=0, tiled=True)  26.2 us
    unnamed x28, local copies, waits for them, and re-layouts  19.4 us
    all_to_all x1, starting transfers between devices, shards(): lax.all_to_all(copies, ('zh', 'y'), split_axis=0, concat_axis=0, tiled=True)  13 us
  transfers between devices with their start and end apart: 4, of which 4 were waited for; matrix products, arithmetic and copies ran while one was open for 4% of the time, Pallas kernels for 0%

profile of v1, /device:TPU:1, one launch (start us, length us, event | category | flops | bytes accessed | tf_op | source)
XLA Modules:
  0.0 349.4 jit_solution(15768023277636630760)
XLA Ops:
  7.2 2.9 reshape.112
  10.1 1.6 copy.54
  11.7 5.1 %all-to-all-start = ((bf16[4,192,1024]{2,1,0:T(8,128)(2,1)}), bf16[4,192,1024]{2,1,0:T(8,128)(2,1)}, u32[]{:S(2)}, u32[]{:S(2)}) async-start(bf16[4,192,1024]{2,1,0:T(8,128)(2,1)} %bitcast.32), calls=%async_computation | async-start | bytes 3145728 | tf_op jit(solution)/shard_map/all_to_all | solution.py:73
  17.1 0.9 reduce-window.6
  18.9 0.5 convolution_convert_fusion
  19.4 1.9 reshape.113
  21.3 1.2 fusion.4
  22.5 0.7 reshape.114
  23.2 0.7 reshape.115
  23.9 0.7 reshape.116
  24.6 1.1 pad_maximum_fusion
  25.8 5.7 %all-to-all-done = bf16[4,192,1024]{2,1,0:T(8,128)(2,1)} async-done(((bf16[4,192,1024]{2,1,0:T(8,128)(2,1)}), bf16[4,192,1024]{2,1,0:T(8,128)(2,1)}, u32[]{:S(2)}, u32[]{:S(2)}) %all-to-all-start) | async-done | bytes 1572896 | tf_op jit(solution)/shard_map/all_to_all | solution.py:73
  31.5 0.5 broadcast.59
  32.0 2.6 reduce.4
  34.6 5.1 %reshape.147 = bf16[64,2,6656]{2,1,0:T(2,128)(2,1)} reshape(bf16[64,13312]{1,0:T(8,128)(2,1)} %reduce.4) | data formatting | bytes 3407872
  39.7 101.9 %all_to_all.35 = bf16[64,2,6656]{2,1,0:T(2,128)(2,1)S(1)} all-to-all(bf16[64,2,6656]{2,1,0:T(2,128)(2,1)} %reshape.147), channel_id=1, replica_groups=mesh['expert'=64,'zh'=2,'y'=4] {'expert'}, dimensions={0} | all-to-all | bytes 3407872 | tf_op jit(solution)/shard_map/all_to_all | solution.py:75
  141.6 3.9 %reshape.148 = bf16[64,1,13312]{2,1,0:T(2,128)(2,1)} reshape(bf16[64,2,6656]{2,1,0:T(2,128)(2,1)S(1)} %all_to_all.35) | data formatting | bytes 3407872
  145.5 2.5 copy.53
  148.0 1.2 copy-done.1
  149.3 2.0 reshape.141
  151.2 4.1 %fusion.16 = f32[4,192,640]{2,1,0:T(8,128)} fusion(bf16[4,192,1024]{2,1,0:T(8,128)(2,1)} %all-to-all-done, bf16[640,1024,1]{1,0,2:T(8,128)(2,1)S(1)} %reshape.141), kind=kOutput, calls=%fused_computation.49 | convolution fusion | flops 1006632960 | bytes 4849664 | tf_op jit(solution)/shard_map/dot_general | solution.py:78
  155.4 30.9 %reduce-scatter.2.cloned.1.call-done = f32[1,192,640]{2,1,0:T(8,128)} async-done(((f32[4,192,640]{2,1,0:T(8,128)}), f32[1,192,640]{2,1,0:T(8,128)}) %reduce-scatter.2.cloned.1.call-update) | async-done | bytes 491536 | tf_op jit(solution)/shard_map/reduce_scatter | solution.py:81
  186.3 1.1 fusion.15
  187.5 1.0 broadcast_in_dim.36
  188.6 6.6 %reduce.5 = bf16[8,61440]{1,0:T(8,128)(2,1)S(1)} reduce(bf16[8,1,61440]{2,1,0:T(2,128)(2,1)S(1)} %broadcast_in_dim.36, bf16[]{:T(256)} %broadcast.59), dimensions={1}, to_apply=%broadcast_in_dim.36.reduce_sub_computation | reduce | bytes 1966082 | tf_op jit(solution)/shard_map/broadcast_in_dim | solution.py:84
  195.2 1.8 reshape.149
  197.0 13.0 %all-to-all-start.2 = ((bf16[8,2,30720]{2,1,0:T(2,128)(2,1)}), bf16[8,2,30720]{2,1,0:T(2,128)(2,1)S(1)}, u32[]{:S(2)}, u32[]{:S(2)}) async-start(bf16[8,2,30720]{2,1,0:T(2,128)(2,1)} %reshape.149), calls=%async_computation.3 | async-start | bytes 1966080 | tf_op jit(solution)/shard_map/all_to_all | solution.py:85
  210.0 1.0 slice.71
  211.0 0.8 gather_fusion
  211.8 0.9 broadcast_select_fusion
  212.7 31.5 %all-to-all-done.2 = bf16[8,2,30720]{2,1,0:T(2,128)(2,1)S(1)} async-done(((bf16[8,2,30720]{2,1,0:T(2,128)(2,1)}), bf16[8,2,30720]{2,1,0:T(2,128)(2,1)S(1)}, u32[]{:S(2)}, u32[]{:S(2)}) %all-to-all-start.2) | async-done | bytes 983072 | tf_op jit(solution)/shard_map/all_to_all | solution.py:85
  244.1 1.0 reshape.150
  245.1 6.0 %reduce.2 = bf16[8,61440]{1,0:T(8,128)(2,1)S(1)} reduce(bf16[8,1,61440]{2,1,0:T(2,128)(2,1)S(1)} %reshape.150, bf16[]{:T(256)} %constant.70), dimensions={1}, to_apply=%all_to_all.27.reduce_sub_computation | reduce | bytes 1966082 | tf_op jit(solution)/shard_map/all_to_all | solution.py:85
  251.6 0.6 slice-done
  252.2 1.5 convolution_convert_fusion.1
  253.7 1.9 reshape.120
  255.7 1.4 reduce.6
  257.2 1.6 reshape.151
  258.8 26.2 %all-to-all-start.3 = ((bf16[64,2,4096]{2,1,0:T(2,128)(2,1)}), bf16[64,2,4096]{2,1,0:T(2,128)(2,1)S(1)}, u32[]{:S(2)}, u32[]{:S(2)}) async-start(bf16[64,2,4096]{2,1,0:T(2,128)(2,1)} %reshape.151), calls=%async_computation.4 | async-start | bytes 2097152 | tf_op jit(solution)/shard_map/all_to_all | solution.py:93
  285.1 1.0 select_reduce_fusion
  286.0 50.2 %all-to-all-done.3 = bf16[64,2,4096]{2,1,0:T(2,128)(2,1)S(1)} async-done(((bf16[64,2,4096]{2,1,0:T(2,128)(2,1)}), bf16[64,2,4096]{2,1,0:T(2,128)(2,1)S(1)}, u32[]{:S(2)}, u32[]{:S(2)}) %all-to-all-start.3) | async-done | bytes 1048608 | tf_op jit(solution)/shard_map/all_to_all | solution.py:93
  336.2 1.0 reshape.152
  337.3 1.1 copy.55
  338.6 0.8 reshape.121
  339.3 0.7 reshape.129
  340.1 0.7 reshape.131
  340.8 0.7 reshape.122
  341.5 1.0 convolution_convert_fusion.2
  (43 shorter events, 2.0 us)
Async XLA Ops:
  7.2 11.7 %copy-start = (bf16[40,4096]{1,0:T(8,128)(2,1)S(1)}, bf16[40,4096]{1,0:T(8,128)(2,1)}, u32[]{:S(2)}) copy-start(bf16[40,4096]{1,0:T(8,128)(2,1)} %param.9) | copy-start | bytes 983044
  11.7 5.1 %copy-start.6 = (s32[40,8]{0,1:T(8,128)S(1)}, s32[40,8]{0,1:T(8,128)}, u32[]{:S(2)}) copy-start(s32[40,8]{0,1:T(8,128)} %param.10) | copy-start | bytes 3844
  11.7 19.8 %all-to-all-start = ((bf16[4,192,1024]{2,1,0:T(8,128)(2,1)}), bf16[4,192,1024]{2,1,0:T(8,128)(2,1)}, u32[]{:S(2)}, u32[]{:S(2)}) async-start(bf16[4,192,1024]{2,1,0:T(8,128)(2,1)} %bitcast.32), calls=%async_computation | async-start | bytes 3145728 | tf_op jit(solution)/shard_map/all_to_all | solution.py:73
  16.9 169.4 %reduce-scatter.2.cloned.1.call-start = ((), (), s32[]{:S(2)}) async-start(), calls=%async_computation.5 | async-start | bytes 2457600 | tf_op jit(solution)/shard_map/reduce_scatter | solution.py:81
  18.8 2.4 copy-start.4
  18.8 2.4 copy-start.5
  148.0 1.2 copy-start.1
  197.0 13.0 %copy-start.8 = (s32[64]{0:T(128)S(1)}, s32[64]{0:T(128)}, u32[]{:S(2)}) copy-start(s32[64]{0:T(128)} %param.12) | copy-start | bytes 772
  197.0 47.1 %all-to-all-start.2 = ((bf16[8,2,30720]{2,1,0:T(2,128)(2,1)}), bf16[8,2,30720]{2,1,0:T(2,128)(2,1)S(1)}, u32[]{:S(2)}, u32[]{:S(2)}) async-start(bf16[8,2,30720]{2,1,0:T(2,128)(2,1)} %reshape.149), calls=%async_computation.3 | async-start | bytes 1966080 | tf_op jit(solution)/shard_map/all_to_all | solution.py:85
  251.1 1.1 slice-start
  252.2 3.4 copy-start.2
  257.2 27.8 %copy-start.7 = (f32[40,8]{0,1:T(8,128)S(1)}, f32[40,8]{0,1:T(8,128)}, u32[]{:S(2)}) copy-start(f32[40,8]{0,1:T(8,128)} %param.11) | copy-start | bytes 3844
  258.8 77.5 %all-to-all-start.3 = ((bf16[64,2,4096]{2,1,0:T(2,128)(2,1)}), bf16[64,2,4096]{2,1,0:T(2,128)(2,1)S(1)}, u32[]{:S(2)}, u32[]{:S(2)}) async-start(bf16[64,2,4096]{2,1,0:T(2,128)(2,1)} %reshape.151), calls=%async_computation.4 | async-start | bytes 2097152 | tf_op jit(solution)/shard_map/all_to_all | solution.py:93
  338.5 3.0 copy-start.3
Sparse Core Ops, SparseCore 0:
  155.5 30.7 reduce-scatter.1

commit v2 on v1

--- a/solution.py
+++ b/solution.py
@@ -69,9 +69,8 @@
     outgoing = jnp.concatenate([outgoing.reshape(groups, capacity * quarter)] + list(pieces), axis=1)
     joined = gate_up.reshape(-1, quarters, quarter)
     hidden_count = joined.shape[0] // 2
-    by_quarter = jnp.moveaxis(joined, 1, 0)
-    quarter_weights = lax.all_to_all(by_quarter, "y", split_axis=0, concat_axis=0, tiled=True)
-    quarter_weights, outgoing = lax.optimization_barrier((quarter_weights, outgoing))
+    every_weight = lax.all_gather(gate_up.reshape(-1, model_width), "y", axis=0, tiled=False)
+    quarter_weights = lax.dynamic_slice_in_dim(every_weight, lax.axis_index("y") * quarter, quarter, axis=2)
     received = lax.all_to_all(outgoing, "expert", split_axis=0, concat_axis=0, tiled=True)
     spread = received[:, capacity * quarter :]
     received = received[:, : capacity * quarter].reshape(groups * capacity, quarter)

time: 350 us -> 332 us (0.949)
  blocking collectives: 102 us -> 96.1 us
  starting transfers between devices: 44.2 us -> 39.2 us
  local copies, waits for them, and re-layouts: 40.8 us -> 37.1 us
    all_to_all x1, blocking collectives: 102 us -> 96.1 us  [shards(): lax.all_to_all(outgoing, 'expert', split_axis=0, concat_axis=0, tiled=True)]
    all_to_all x1 -> x0, waiting for transfers between devices: 5.73 us -> none  [shards(): lax.all_to_all(by_quarter, 'y', split_axis=0, concat_axis=0, tiled=True)]
    all_to_all x1 -> x0, starting transfers between devices: 5.13 us -> none  [shards(): lax.all_to_all(by_quarter, 'y', split_axis=0, concat_axis=0, tiled=True)]
    reshape x2 -> x0, local copies, waits for them, and re-layouts: 4.55 us -> none  [shards(): joined = gate_up.reshape(-1, quarters, quarter)]
    unnamed x28 -> x30, local copies, waits for them, and re-layouts: 19.4 us -> 20.3 us
  transfers between devices with their start and end apart: 4 -> 4, of which waited for: 4 -> 3; matrix products, arithmetic and copies ran while one was open for 4% -> 9% of each run, Pallas kernels for 0% -> 0%
where the time goes in v2:
time: 332 us; the launch traced here: 331 us
  waiting for transfers between devices  115 us (35%)
  blocking collectives  96.1 us (29%)
  starting transfers between devices  39.2 us (12%)
  local copies, waits for them, and re-layouts  37.1 us (11%)
  other arithmetic  21.5 us (6%)
  between operations  14.4 us (4%)
  matrix products  7.22 us (2%)
    all_to_all x1, blocking collectives, shards(): lax.all_to_all(outgoing, 'expert', split_axis=0, concat_axis=0, tiled=True)  96.1 us
    all_to_all x1, waiting for transfers between devices, shards(): lax.all_to_all(results, 'expert', split_axis=0, concat_axis=0, tiled=True)  50.2 us
    reduce_scatter x1, waiting for transfers between devices, shards(): projected = lax.psum_scatter(partial, 'y', scatter_dimension=0, tiled=False)  33 us
    all_to_all x1, waiting for transfers between devices, shards(): lax.all_to_all(copies, ('zh', 'y'), split_axis=0, concat_axis=0, tiled=True)  31.4 us
    all_to_all x1, starting transfers between devices, shards(): lax.all_to_all(results, 'expert', split_axis=0, concat_axis=0, tiled=True)  26.2 us
    unnamed x30, local copies, waits for them, and re-layouts  20.3 us
    all_to_all x1, starting transfers between devices, shards(): lax.all_to_all(copies, ('zh', 'y'), split_axis=0, concat_axis=0, tiled=True)  12.9 us
  transfers between devices with their start and end apart: 4, of which 3 were waited for; matrix products, arithmetic and copies ran while one was open for 9% of the time, Pallas kernels for 0%

profile of v2, /device:TPU:1, one launch (start us, length us, event | category | flops | bytes accessed | tf_op | source)
XLA Modules:
  0.0 331.0 jit_solution(14967862149014586461)
XLA Ops:
  7.3 0.7 all-gather.2.cloned.1.call-update
  8.0 0.8 copy.32
  8.9 0.9 reduce-window.6
  10.3 0.3 fusion.6
  10.6 0.7 reshape.112
  11.3 0.7 reshape.111
  12.0 0.7 reshape.110
  12.7 0.3 convert_reduce_fusion
  13.0 0.5 convolution_convert_fusion
  13.6 1.9 reshape.109
  15.5 1.1 maximum_bitcast_fusion
  16.6 0.5 broadcast.59
  17.1 2.6 reduce.4
  19.7 5.1 %reshape.143 = bf16[64,2,6656]{2,1,0:T(2,128)(2,1)} reshape(bf16[64,13312]{1,0:T(8,128)(2,1)} %reduce.4) | data formatting | bytes 3407872
  24.8 96.1 %all_to_all.30 = bf16[64,2,6656]{2,1,0:T(2,128)(2,1)S(1)} all-to-all(bf16[64,2,6656]{2,1,0:T(2,128)(2,1)} %reshape.143), channel_id=1, replica_groups=mesh['expert'=64,'zh'=2,'y'=4] {'expert'}, dimensions={0} | all-to-all | bytes 3407872 | tf_op jit(solution)/shard_map/all_to_all | solution.py:74
  120.9 3.9 %reshape.144 = bf16[64,1,13312]{2,1,0:T(2,128)(2,1)} reshape(bf16[64,2,6656]{2,1,0:T(2,128)(2,1)S(1)} %all_to_all.30) | data formatting | bytes 3407872
  124.9 2.5 copy.47
  127.4 1.3 copy-done.1
  128.8 2.0 reshape.137
  130.8 4.1 %fusion = f32[4,192,640]{2,1,0:T(8,128)} fusion(bf16[640,1024,1]{1,0,2:T(8,128)(2,1)S(1)} %reshape.137, bf16[4,192,4096]{2,1,0:T(8,128)(2,1)} %all-gather.2.cloned.1.call-done, s32[]{:T(128)S(6)} %select_n.18), kind=kOutput, calls=%fused_computation.4 | convolution fusion | flops 1006632960 | bytes 4849668 | tf_op jit(solution)/shard_map/dot_general | solution.py:77
  134.9 33.0 %reduce-scatter.2.cloned.1.call-done = f32[1,192,640]{2,1,0:T(8,128)} async-done(((f32[4,192,640]{2,1,0:T(8,128)}), f32[1,192,640]{2,1,0:T(8,128)}) %reduce-scatter.2.cloned.1.call-update) | async-done | bytes 491536 | tf_op jit(solution)/shard_map/reduce_scatter | solution.py:80
  167.9 1.1 fusion.18
  169.2 1.0 broadcast_in_dim.36
  170.2 6.6 %reduce.5 = bf16[8,61440]{1,0:T(8,128)(2,1)S(1)} reduce(bf16[8,1,61440]{2,1,0:T(2,128)(2,1)S(1)} %broadcast_in_dim.36, bf16[]{:T(256)} %broadcast.59), dimensions={1}, to_apply=%broadcast_in_dim.36.reduce_sub_computation | reduce | bytes 1966082 | tf_op jit(solution)/shard_map/broadcast_in_dim | solution.py:83
  176.8 1.8 reshape.145
  178.6 12.9 %all-to-all-start.1 = ((bf16[8,2,30720]{2,1,0:T(2,128)(2,1)}), bf16[8,2,30720]{2,1,0:T(2,128)(2,1)S(1)}, u32[]{:S(2)}, u32[]{:S(2)}) async-start(bf16[8,2,30720]{2,1,0:T(2,128)(2,1)} %reshape.145), calls=%async_computation.2 | async-start | bytes 1966080 | tf_op jit(solution)/shard_map/all_to_all | solution.py:84
  191.6 1.0 slice.71
  192.6 0.8 gather_fusion
  193.4 0.9 broadcast_select_fusion
  194.2 31.4 %all-to-all-done.1 = bf16[8,2,30720]{2,1,0:T(2,128)(2,1)S(1)} async-done(((bf16[8,2,30720]{2,1,0:T(2,128)(2,1)}), bf16[8,2,30720]{2,1,0:T(2,128)(2,1)S(1)}, u32[]{:S(2)}, u32[]{:S(2)}) %all-to-all-start.1) | async-done | bytes 983072 | tf_op jit(solution)/shard_map/all_to_all | solution.py:84
  225.7 1.0 reshape.146
  226.7 6.0 %reduce.2 = bf16[8,61440]{1,0:T(8,128)(2,1)S(1)} reduce(bf16[8,1,61440]{2,1,0:T(2,128)(2,1)S(1)} %reshape.146, bf16[]{:T(256)} %constant.70), dimensions={1}, to_apply=%all_to_all.23.reduce_sub_computation | reduce | bytes 1966082 | tf_op jit(solution)/shard_map/all_to_all | solution.py:84
  232.7 0.4 reshape.114
  233.1 0.6 slice-done
  233.8 1.5 convolution_convert_fusion.1
  235.3 1.9 reshape.116
  237.3 1.4 reduce.6
  238.7 1.6 reshape.147
  240.3 26.2 %all-to-all-start.2 = ((bf16[64,2,4096]{2,1,0:T(2,128)(2,1)}), bf16[64,2,4096]{2,1,0:T(2,128)(2,1)S(1)}, u32[]{:S(2)}, u32[]{:S(2)}) async-start(bf16[64,2,4096]{2,1,0:T(2,128)(2,1)} %reshape.147), calls=%async_computation.3 | async-start | bytes 2097152 | tf_op jit(solution)/shard_map/all_to_all | solution.py:92
  266.6 1.0 select_reduce_fusion
  267.6 50.2 %all-to-all-done.2 = bf16[64,2,4096]{2,1,0:T(2,128)(2,1)S(1)} async-done(((bf16[64,2,4096]{2,1,0:T(2,128)(2,1)}), bf16[64,2,4096]{2,1,0:T(2,128)(2,1)S(1)}, u32[]{:S(2)}, u32[]{:S(2)}) %all-to-all-start.2) | async-done | bytes 1048608 | tf_op jit(solution)/shard_map/all_to_all | solution.py:92
  317.8 1.0 reshape.148
  318.9 1.1 copy.48
  320.2 0.8 reshape.117
  320.9 0.7 reshape.118
  321.6 0.7 reshape.125
  322.4 0.7 reshape.127
  323.1 1.0 convolution_convert_fusion.2
  (44 shorter events, 1.2 us)
Async XLA Ops:
  7.2 5.9 %copy-start = (bf16[40,4096]{1,0:T(8,128)(2,1)S(1)}, bf16[40,4096]{1,0:T(8,128)(2,1)}, u32[]{:S(2)}) copy-start(bf16[40,4096]{1,0:T(8,128)(2,1)} %param.9) | copy-start | bytes 983044
  7.2 3.1 copy-start.7
  7.2 3.1 copy-start.5
  7.2 3.1 copy-start.6
  7.2 3.1 copy-start.3
  7.2 123.5 %all-gather.2.cloned.1.call-start = ((), (), s32[]{:S(2)}) async-start(), calls=%async_computation.4 | async-start | bytes 7864320 | tf_op jit(solution)/shard_map/all_gather | solution.py:72
  8.0 160.0 %reduce-scatter.2.cloned.1.call-start = ((), (), s32[]{:S(2)}) async-start(), calls=%async_computation.5 | async-start | bytes 2457600 | tf_op jit(solution)/shard_map/reduce_scatter | solution.py:80
  127.4 1.3 copy-start.1
  178.6 12.9 %copy-start.9 = (s32[64]{0:T(128)S(1)}, s32[64]{0:T(128)}, u32[]{:S(2)}) copy-start(s32[64]{0:T(128)} %param.12) | copy-start | bytes 772
  178.6 47.1 %all-to-all-start.1 = ((bf16[8,2,30720]{2,1,0:T(2,128)(2,1)}), bf16[8,2,30720]{2,1,0:T(2,128)(2,1)S(1)}, u32[]{:S(2)}, u32[]{:S(2)}) async-start(bf16[8,2,30720]{2,1,0:T(2,128)(2,1)} %reshape.145), calls=%async_computation.2 | async-start | bytes 1966080 | tf_op jit(solution)/shard_map/all_to_all | solution.py:84
  232.7 1.1 slice-start
  233.8 3.4 %copy-start.2 = (bf16[64,3072]{1,0:T(8,128)(2,1)S(1)}, bf16[64,3072]{1,0:T(8,128)(2,1)}, u32[]{:S(2)}) copy-start(bf16[64,3072]{1,0:T(8,128)(2,1)} %broadcast_select_fusion) | copy-start | bytes 1179652
  238.7 27.8 %copy-start.8 = (f32[40,8]{0,1:T(8,128)S(1)}, f32[40,8]{0,1:T(8,128)}, u32[]{:S(2)}) copy-start(f32[40,8]{0,1:T(8,128)} %param.11) | copy-start | bytes 3844
  240.3 77.5 %all-to-all-start.2 = ((bf16[64,2,4096]{2,1,0:T(2,128)(2,1)}), bf16[64,2,4096]{2,1,0:T(2,128)(2,1)S(1)}, u32[]{:S(2)}, u32[]{:S(2)}) async-start(bf16[64,2,4096]{2,1,0:T(2,128)(2,1)} %reshape.147), calls=%async_computation.3 | async-start | bytes 2097152 | tf_op jit(solution)/shard_map/all_to_all | solution.py:92
  320.1 3.0 copy-start.4
Sparse Core Ops, SparseCore 0:
  10.1 78.4 all-gather.1
  135.1 32.8 reduce-scatter.1

commit v3 on v2

--- a/solution.py
+++ b/solution.py
@@ -79,19 +79,15 @@
     )
     projected = lax.psum_scatter(partial, "y", scatter_dimension=0, tiled=False)
     hidden = (jax.nn.silu(projected[:hidden_count]) * projected[hidden_count:]).astype(jnp.bfloat16)
-    shard_count = lax.axis_size(("zh", "y"))
-    copies = jnp.broadcast_to(hidden.reshape(1, -1), (shard_count, hidden.size))
-    every_hidden = lax.all_to_all(copies, ("zh", "y"), split_axis=0, concat_axis=0, tiled=True)
-    every_hidden = every_hidden.reshape(shard_count * hidden_count, -1)
+    back = lax.all_to_all(jnp.take(spread, partner, axis=0), "expert", split_axis=0, concat_axis=0, tiled=True)
+    every_hidden = lax.all_gather(hidden, ("zh", "y"), axis=0, tiled=False)
+    every_hidden = every_hidden.reshape(-1, hidden.shape[1])
     down_rows = down_new.reshape(-1, part_width)
     summed = lax.dot_general(
         every_hidden, down_rows, (((0,), (0,)), ((), ())), preferred_element_type=jnp.float32
     )
     results = summed.astype(jnp.bfloat16).reshape(groups, capacity * part_width)
-    results = jnp.concatenate([results, jnp.take(spread, partner, axis=0)], axis=1)
     returned = lax.all_to_all(results, "expert", split_axis=0, concat_axis=0, tiled=True)
-    back = returned[:, capacity * part_width :]
-    returned = returned[:, : capacity * part_width]
     widths = [p.shape[1] for p in pieces]
     rows_out = back[:, : widths[0]].reshape(new_rows.shape)
     first_out = back[:, widths[0] : widths[0] + widths[1]].astype(jnp.float32).reshape(first_new.shape)

time: 332 us -> 325 us (0.979)
  blocking collectives: 96.1 us -> 166 us
  waiting for transfers between devices: 115 us -> 53.3 us
  local copies, waits for them, and re-layouts: 37.1 us -> 28.4 us
  other arithmetic: 21.5 us -> 17.4 us
    all_gather x0 -> x1, blocking collectives: none -> 69.9 us  [shards(): every_hidden = lax.all_gather(hidden, ('zh', 'y'), axis=0, tiled=False)]
    all_to_all x1, waiting for transfers between devices: 31.4 us -> 0.01 us  [shards(): lax.all_to_all(jnp.take(spread, partner, axis=0), 'expert', split_axis=0,...]
    all_to_all x1, waiting for transfers between devices: 50.2 us -> 31.5 us  [shards(): lax.all_to_all(results, 'expert', split_axis=0, concat_axis=0, tiled=True)]
    reduce_scatter x1, waiting for transfers between devices: 33 us -> 21 us  [shards(): projected = lax.psum_scatter(partial, 'y', scatter_dimension=0, tiled=False)]
    all_to_all x2, other arithmetic: 1.51 us -> 8.5 us  [shards(): lax.all_to_all(results, 'expert', split_axis=0, concat_axis=0, tiled=True)]
    broadcast_in_dim x1 -> x0, other arithmetic: 6.63 us -> none  [shards(): copies = jnp.broadcast_to(hidden.reshape(1, -1), (shard_count, hidden.size))]
    all_to_all x1 -> x0, other arithmetic: 5.99 us -> none  [shards(): lax.all_to_all(copies, ('zh', 'y'), split_axis=0, concat_axis=0, tiled=True)]
    all_to_all x1, starting transfers between devices: 12.9 us -> 8.43 us  [shards(): lax.all_to_all(jnp.take(spread, partner, axis=0), 'expert', split_axis=0,...]
  transfers between devices with their start and end apart: 4 -> 4, of which waited for: 3 -> 2; matrix products, arithmetic and copies ran while one was open for 9% -> 13% of each run, Pallas kernels for 0% -> 0%
where the time goes in v3:
time: 325 us; the launch traced here: 324 us
  blocking collectives  166 us (51%)
  waiting for transfers between devices  53.3 us (16%)
  starting transfers between devices  37.9 us (12%)
  local copies, waits for them, and re-layouts  28.4 us (9%)
  other arithmetic  17.4 us (5%)
  between operations  14.3 us (4%)
  matrix products  6.77 us (2%)
    all_to_all x1, blocking collectives, shards(): lax.all_to_all(outgoing, 'expert', split_axis=0, concat_axis=0, tiled=True)  96.1 us
    all_gather x1, blocking collectives, shards(): every_hidden = lax.all_gather(hidden, ('zh', 'y'), axis=0, tiled=False)  69.9 us
    all_to_all x1, waiting for transfers between devices, shards(): lax.all_to_all(results, 'expert', split_axis=0, concat_axis=0, tiled=True)  31.5 us
    all_to_all x1, starting transfers between devices, shards(): lax.all_to_all(results, 'expert', split_axis=0, concat_axis=0, tiled=True)  29.4 us
    reduce_scatter x1, waiting for transfers between devices, shards(): projected = lax.psum_scatter(partial, 'y', scatter_dimension=0, tiled=False)  21 us
    unnamed x20, local copies, waits for them, and re-layouts  16.4 us
    all_to_all x2, other arithmetic, shards(): lax.all_to_all(results, 'expert', split_axis=0, concat_axis=0, tiled=True)  8.5 us
    all_to_all x1, starting transfers between devices, shards(): lax.all_to_all(jnp.take(spread, partner, axis=0), 'expert', split_axis=0,...  8.43 us
  transfers between devices with their start and end apart: 4, of which 2 were waited for; matrix products, arithmetic and copies ran while one was open for 13% of the time, Pallas kernels for 0%

profile of v3, /device:TPU:1, one launch (start us, length us, event | category | flops | bytes accessed | tf_op | source)
XLA Modules:
  0.0 324.1 jit_solution(14993748734050044063)
XLA Ops:
  7.2 0.7 all-gather.2.cloned.1.call-update
  8.0 0.8 copy.35
  8.7 0.1 eq.37
  8.9 0.9 reduce-window.6
  9.8 0.2 slice_reduce_fusion
  10.0 0.1 bitcast_bitcast_fusion
  10.3 0.3 convert_reduce_fusion
  10.6 0.5 convolution_convert_fusion
  11.2 1.9 reshape.109
  13.1 1.2 fusion.6
  14.3 0.7 reshape.110
  15.0 0.7 reshape.111
  15.7 0.7 reshape.112
  16.4 1.1 maximum_bitcast_fusion
  17.6 0.5 broadcast.70
  18.1 2.6 reduce.4
  20.7 5.1 %reshape.142 = bf16[64,2,6656]{2,1,0:T(2,128)(2,1)} reshape(bf16[64,13312]{1,0:T(8,128)(2,1)} %reduce.4) | data formatting | bytes 3407872
  25.8 96.1 %all_to_all.31 = bf16[64,2,6656]{2,1,0:T(2,128)(2,1)S(1)} all-to-all(bf16[64,2,6656]{2,1,0:T(2,128)(2,1)} %reshape.142), channel_id=1, replica_groups=mesh['expert'=64,'zh'=2,'y'=4] {'expert'}, dimensions={0} | all-to-all | bytes 3407872 | tf_op jit(solution)/shard_map/all_to_all | solution.py:74
  121.9 3.9 %reshape.143 = bf16[64,1,13312]{2,1,0:T(2,128)(2,1)} reshape(bf16[64,2,6656]{2,1,0:T(2,128)(2,1)S(1)} %all_to_all.31) | data formatting | bytes 3407872
  125.8 2.5 copy.51
  128.3 0.1 slice.54
  128.4 2.9 reshape.136
  131.3 4.5 %fusion = f32[4,192,640]{2,1,0:T(8,128)} fusion(bf16[640,1024,1]{1,0,2:T(8,128)(2,1)} %reshape.136, bf16[4,192,4096]{2,1,0:T(8,128)(2,1)} %all-gather.2.cloned.1.call-done, s32[]{:T(128)S(6)} %select_n.25), kind=kOutput, calls=%fused_computation.4 | convolution fusion | flops 1006632960 | bytes 4849668 | tf_op jit(solution)/shard_map/dot_general | solution.py:77
  135.8 0.6 copy-done.4
  136.5 0.8 gather_fusion
  137.3 0.1 bitcast_select_fusion
  137.4 0.9 reduce.6
  138.3 1.0 reshape.146
  139.4 8.4 %all-to-all-start.2 = ((bf16[64,2,1536]{2,1,0:T(2,128)(2,1)}), bf16[64,2,1536]{2,1,0:T(2,128)(2,1)S(1)}, u32[]{:S(2)}, u32[]{:S(2)}) async-start(bf16[64,2,1536]{2,1,0:T(2,128)(2,1)} %reshape.146), calls=%async_computation.3 | async-start | bytes 786432 | tf_op jit(solution)/shard_map/all_to_all | solution.py:82
  147.8 21.0 %reduce-scatter.2.cloned.1.call-done = f32[1,192,640]{2,1,0:T(8,128)} async-done(((f32[4,192,640]{2,1,0:T(8,128)}), f32[1,192,640]{2,1,0:T(8,128)}) %reduce-scatter.2.cloned.1.call-update) | async-done | bytes 491536 | tf_op jit(solution)/shard_map/reduce_scatter | solution.py:80
  168.8 1.1 fusion.9
  170.0 69.9 %all_gather.8 = bf16[8,96,640]{2,1,0:T(8,128)(2,1)S(1)} all-gather(bf16[1,96,640]{2,1,0:T(8,128)(2,1)S(1)} %fusion.9), channel_id=1, replica_groups=mesh['expert'=64,'zh'=2,'y'=4] {'zh','y'}, dimensions={0}, use_global_device_ids=true | all-gather | bytes 1105920 | tf_op jit(solution)/shard_map/all_gather | solution.py:83
  239.9 0.7 convolution_convert_fusion.1
  240.6 0.4 all_to_all.27
  241.0 4.6 %reduce.5 = bf16[64,5120]{1,0:T(8,128)(2,1)S(1)} reduce(bf16[64,1,5120]{2,1,0:T(2,128)(2,1)S(1)} %all_to_all.27, bf16[]{:T(256)} %broadcast.70), dimensions={1}, to_apply=%all_to_all.27.reduce_sub_computation | reduce | bytes 1310722 | tf_op jit(solution)/shard_map/all_to_all | solution.py:90
  245.6 1.3 reshape.144
  246.9 29.4 %all-to-all-start.1 = ((bf16[64,2,2560]{2,1,0:T(2,128)(2,1)}), bf16[64,2,2560]{2,1,0:T(2,128)(2,1)S(1)}, u32[]{:S(2)}, u32[]{:S(2)}) async-start(bf16[64,2,2560]{2,1,0:T(2,128)(2,1)} %reshape.144), calls=%async_computation.2 | async-start | bytes 1310720 | tf_op jit(solution)/shard_map/all_to_all | solution.py:90
  276.4 0.3 select_reduce_fusion
  276.7 0.3 reshape.147
  277.0 0.1 copy.52
  277.2 0.7 reshape.124
  278.0 0.7 reshape.126
  278.7 0.7 reshape.117
  279.4 31.5 %all-to-all-done.1 = bf16[64,2,2560]{2,1,0:T(2,128)(2,1)S(1)} async-done(((bf16[64,2,2560]{2,1,0:T(2,128)(2,1)}), bf16[64,2,2560]{2,1,0:T(2,128)(2,1)S(1)}, u32[]{:S(2)}, u32[]{:S(2)}) %all-to-all-start.1) | async-done | bytes 655392 | tf_op jit(solution)/shard_map/all_to_all | solution.py:90
  310.9 0.5 reshape.145
  311.5 3.9 %reduce.2 = bf16[64,5120]{1,0:T(8,128)(2,1)S(1)} reduce(bf16[64,1,5120]{2,1,0:T(2,128)(2,1)S(1)} %reshape.145, bf16[]{:T(256)} %constant.70), dimensions={1}, to_apply=%all_to_all.24.reduce_sub_computation | reduce | bytes 1310722 | tf_op jit(solution)/shard_map/all_to_all | solution.py:90
  315.4 0.8 reshape.116
  316.2 1.0 convolution_convert_fusion.2
  (28 shorter events, 0.5 us)
Async XLA Ops:
  7.2 3.4 %copy-start = (bf16[40,4096]{1,0:T(8,128)(2,1)S(1)}, bf16[40,4096]{1,0:T(8,128)(2,1)}, u32[]{:S(2)}) copy-start(bf16[40,4096]{1,0:T(8,128)(2,1)} %param.9) | copy-start | bytes 983044
  7.2 124.1 %all-gather.2.cloned.1.call-start = ((), (), s32[]{:S(2)}) async-start(), calls=%async_computation.4 | async-start | bytes 7864320 | tf_op jit(solution)/shard_map/all_gather | solution.py:72
  7.9 160.9 %reduce-scatter.2.cloned.1.call-start = ((), (), s32[]{:S(2)}) async-start(), calls=%async_computation.5 | async-start | bytes 2457600 | tf_op jit(solution)/shard_map/reduce_scatter | solution.py:80
  10.6 2.4 copy-start.1
  10.6 2.4 copy-start.2
  135.8 0.7 copy-start.4
  139.4 107.6 %all-to-all-start.2 = ((bf16[64,2,1536]{2,1,0:T(2,128)(2,1)}), bf16[64,2,1536]{2,1,0:T(2,128)(2,1)S(1)}, u32[]{:S(2)}, u32[]{:S(2)}) async-start(bf16[64,2,1536]{2,1,0:T(2,128)(2,1)} %reshape.146), calls=%async_computation.3 | async-start | bytes 786432 | tf_op jit(solution)/shard_map/all_to_all | solution.py:82
  147.8 92.1 %slice-start = ((bf16[1,768,512]{2,1,0:T(8,128)(2,1)}), bf16[1,640,512]{2,1,0:T(8,128)(2,1)S(1)}, s32[]{:S(2)}) async-start(bf16[1,768,512]{2,1,0:T(8,128)(2,1)} %param.14), calls=%async_computation.6 | async-start | bytes 1310720 | tf_op jit(solution)/shard_map/slice | solution.py:51
  245.6 30.7 %copy-start.3 = (f32[40,8]{0,1:T(8,128)S(1)}, f32[40,8]{0,1:T(8,128)}, u32[]{:S(2)}) copy-start(f32[40,8]{0,1:T(8,128)} %param.11) | copy-start | bytes 3844
  246.9 64.0 %all-to-all-start.1 = ((bf16[64,2,2560]{2,1,0:T(2,128)(2,1)}), bf16[64,2,2560]{2,1,0:T(2,128)(2,1)S(1)}, u32[]{:S(2)}, u32[]{:S(2)}) async-start(bf16[64,2,2560]{2,1,0:T(2,128)(2,1)} %reshape.144), calls=%async_computation.2 | async-start | bytes 1310720 | tf_op jit(solution)/shard_map/all_to_all | solution.py:90
Sparse Core Ops, SparseCore 0:
  10.1 78.4 all-gather.1
  136.0 32.8 reduce-scatter.1

commit v4 on v3

--- a/solution.py
+++ b/solution.py
@@ -80,7 +80,7 @@
     projected = lax.psum_scatter(partial, "y", scatter_dimension=0, tiled=False)
     hidden = (jax.nn.silu(projected[:hidden_count]) * projected[hidden_count:]).astype(jnp.bfloat16)
     back = lax.all_to_all(jnp.take(spread, partner, axis=0), "expert", split_axis=0, concat_axis=0, tiled=True)
-    every_hidden = lax.all_gather(hidden, ("zh", "y"), axis=0, tiled=False)
+    every_hidden = lax.all_gather(lax.all_gather(hidden, "y", axis=0, tiled=False), "zh", axis=0, tiled=False)
     every_hidden = every_hidden.reshape(-1, hidden.shape[1])
     down_rows = down_new.reshape(-1, part_width)
     summed = lax.dot_general(

time: 325 us -> 302 us (0.929)
  blocking collectives: 166 us -> 132 us
  starting transfers between devices: 37.9 us -> 49.4 us
    all_gather x1 -> x2, blocking collectives: 69.9 us -> 35.5 us  [the longest x1 25.7 us: shards(): lax.all_gather(lax.all_gather(hidden, 'y', axis=0, tiled=False), 'zh', ax...]
    all_to_all x1, starting transfers between devices: 29.4 us -> 40.9 us  [shards(): lax.all_to_all(results, 'expert', split_axis=0, concat_axis=0, tiled=True)]
  transfers between devices with their start and end apart: 4 -> 4, of which waited for: 2 -> 2; matrix products, arithmetic and copies ran while one was open for 13% -> 14% of each run, Pallas kernels for 0% -> 0%
where the time goes in v4:
time: 302 us; the launch traced here: 301 us
  blocking collectives  132 us (44%)
  waiting for transfers between devices  53.3 us (18%)
  starting transfers between devices  49.4 us (16%)
  local copies, waits for them, and re-layouts  28.4 us (9%)
  other arithmetic  17.4 us (6%)
  between operations  14.3 us (5%)
  matrix products  6.77 us (2%)
    all_to_all x1, blocking collectives, shards(): lax.all_to_all(outgoing, 'expert', split_axis=0, concat_axis=0, tiled=True)  96.1 us
    all_to_all x1, starting transfers between devices, shards(): lax.all_to_all(results, 'expert', split_axis=0, concat_axis=0, tiled=True)  40.9 us
    all_to_all x1, waiting for transfers between devices, shards(): lax.all_to_all(results, 'expert', split_axis=0, concat_axis=0, tiled=True)  31.5 us
    all_gather x1, blocking collectives, shards(): lax.all_gather(lax.all_gather(hidden, 'y', axis=0, tiled=False), 'zh', ax...  25.7 us
    reduce_scatter x1, waiting for transfers between devices, shards(): projected = lax.psum_scatter(partial, 'y', scatter_dimension=0, tiled=False)  21 us
    unnamed x20, local copies, waits for them, and re-layouts  16.4 us
    all_gather x1, blocking collectives, shards(): lax.all_gather(hidden, 'y', axis=0, tiled=False)  9.83 us
    all_to_all x2, other arithmetic, shards(): lax.all_to_all(results, 'expert', split_axis=0, concat_axis=0, tiled=True)  8.5 us
  transfers between devices with their start and end apart: 4, of which 2 were waited for; matrix products, arithmetic and copies ran while one was open for 14% of the time, Pallas kernels for 0%

profile of v4, /device:TPU:1, one launch (start us, length us, event | category | flops | bytes accessed | tf_op | source)
XLA Modules:
  0.0 301.2 jit_solution(8585160449209402535)
XLA Ops:
  7.2 0.7 all-gather.3.cloned.1.call-update
  8.0 0.8 copy.35
  8.7 0.1 eq.37
  8.9 0.9 reduce-window.6
  9.8 0.2 slice_reduce_fusion
  10.0 0.1 bitcast_bitcast_fusion
  10.3 0.3 convert_reduce_fusion
  10.6 0.5 convolution_convert_fusion
  11.2 1.9 reshape.109
  13.1 1.2 fusion.6
  14.3 0.7 reshape.110
  15.0 0.7 reshape.111
  15.7 0.7 reshape.112
  16.4 1.1 maximum_bitcast_fusion
  17.6 0.5 broadcast.70
  18.1 2.6 reduce.4
  20.7 5.1 %reshape.144 = bf16[64,2,6656]{2,1,0:T(2,128)(2,1)} reshape(bf16[64,13312]{1,0:T(8,128)(2,1)} %reduce.4) | data formatting | bytes 3407872
  25.8 96.1 %all_to_all.31 = bf16[64,2,6656]{2,1,0:T(2,128)(2,1)S(1)} all-to-all(bf16[64,2,6656]{2,1,0:T(2,128)(2,1)} %reshape.144), channel_id=1, replica_groups=mesh['expert'=64,'zh'=2,'y'=4] {'expert'}, dimensions={0} | all-to-all | bytes 3407872 | tf_op jit(solution)/shard_map/all_to_all | solution.py:74
  121.9 3.9 %reshape.145 = bf16[64,1,13312]{2,1,0:T(2,128)(2,1)} reshape(bf16[64,2,6656]{2,1,0:T(2,128)(2,1)S(1)} %all_to_all.31) | data formatting | bytes 3407872
  125.8 2.5 copy.51
  128.4 2.9 reshape.138
  131.3 4.5 %fusion = f32[4,192,640]{2,1,0:T(8,128)} fusion(bf16[640,1024,1]{1,0,2:T(8,128)(2,1)} %reshape.138, bf16[4,192,4096]{2,1,0:T(8,128)(2,1)} %all-gather.3.cloned.1.call-done, s32[]{:T(128)S(6)} %select_n.25), kind=kOutput, calls=%fused_computation.4 | convolution fusion | flops 1006632960 | bytes 4849668 | tf_op jit(solution)/shard_map/dot_general | solution.py:77
  135.8 0.6 copy-done.4
  136.5 0.8 gather_fusion
  137.3 0.1 bitcast_select_fusion
  137.4 0.9 reduce.6
  138.3 1.0 reshape.148
  139.4 8.4 %all-to-all-start.2 = ((bf16[64,2,1536]{2,1,0:T(2,128)(2,1)}), bf16[64,2,1536]{2,1,0:T(2,128)(2,1)S(1)}, u32[]{:S(2)}, u32[]{:S(2)}) async-start(bf16[64,2,1536]{2,1,0:T(2,128)(2,1)} %reshape.148), calls=%async_computation.3 | async-start | bytes 786432 | tf_op jit(solution)/shard_map/all_to_all | solution.py:82
  147.8 21.0 %reduce-scatter.2.cloned.1.call-done = f32[1,192,640]{2,1,0:T(8,128)} async-done(((f32[4,192,640]{2,1,0:T(8,128)}), f32[1,192,640]{2,1,0:T(8,128)}) %reduce-scatter.2.cloned.1.call-update) | async-done | bytes 491536 | tf_op jit(solution)/shard_map/reduce_scatter | solution.py:80
  168.8 1.1 fusion.9
  170.0 9.8 %all_gather.14 = bf16[4,96,640]{2,1,0:T(8,128)(2,1)S(1)} all-gather(bf16[1,96,640]{2,1,0:T(8,128)(2,1)S(1)} %fusion.9), channel_id=1, replica_groups=mesh['expert'=64,'zh'=2,'y'=4] {'y'}, dimensions={0}, use_global_device_ids=true | all-gather | bytes 614400 | tf_op jit(solution)/shard_map/all_gather | solution.py:83
  179.8 25.7 %all-gather = bf16[8,96,640]{2,1,0:T(8,128)(2,1)S(1)} all-gather(bf16[4,96,640]{2,1,0:T(8,128)(2,1)S(1)} %all_gather.14), channel_id=2, replica_groups=mesh['expert'=64,'zh'=2,'y'=4] {'zh'}, dimensions={0}, use_global_device_ids=true | all-gather | bytes 1474560 | tf_op jit(solution)/shard_map/all_gather | solution.py:83
  205.5 0.7 convolution_convert_fusion.1
  206.2 0.4 all_to_all.27
  206.6 4.6 %reduce.5 = bf16[64,5120]{1,0:T(8,128)(2,1)S(1)} reduce(bf16[64,1,5120]{2,1,0:T(2,128)(2,1)S(1)} %all_to_all.27, bf16[]{:T(256)} %broadcast.70), dimensions={1}, to_apply=%all_to_all.27.reduce_sub_computation | reduce | bytes 1310722 | tf_op jit(solution)/shard_map/all_to_all | solution.py:90
  211.2 1.3 reshape.146
  212.5 40.9 %all-to-all-start.1 = ((bf16[64,2,2560]{2,1,0:T(2,128)(2,1)}), bf16[64,2,2560]{2,1,0:T(2,128)(2,1)S(1)}, u32[]{:S(2)}, u32[]{:S(2)}) async-start(bf16[64,2,2560]{2,1,0:T(2,128)(2,1)} %reshape.146), calls=%async_computation.2 | async-start | bytes 1310720 | tf_op jit(solution)/shard_map/all_to_all | solution.py:90
  253.5 0.3 select_reduce_fusion
  253.8 0.3 reshape.149
  254.2 0.1 copy.52
  254.4 0.7 reshape.124
  255.1 0.7 reshape.126
  255.9 0.7 reshape.117
  256.6 31.5 %all-to-all-done.1 = bf16[64,2,2560]{2,1,0:T(2,128)(2,1)S(1)} async-done(((bf16[64,2,2560]{2,1,0:T(2,128)(2,1)}), bf16[64,2,2560]{2,1,0:T(2,128)(2,1)S(1)}, u32[]{:S(2)}, u32[]{:S(2)}) %all-to-all-start.1) | async-done | bytes 655392 | tf_op jit(solution)/shard_map/all_to_all | solution.py:90
  288.1 0.5 reshape.147
  288.6 3.9 %reduce.2 = bf16[64,5120]{1,0:T(8,128)(2,1)S(1)} reduce(bf16[64,1,5120]{2,1,0:T(2,128)(2,1)S(1)} %reshape.147, bf16[]{:T(256)} %constant.70), dimensions={1}, to_apply=%all_to_all.24.reduce_sub_computation | reduce | bytes 1310722 | tf_op jit(solution)/shard_map/all_to_all | solution.py:90
  292.6 0.8 reshape.116
  293.3 1.0 convolution_convert_fusion.2
  (29 shorter events, 0.6 us)
Async XLA Ops:
  7.2 3.4 %copy-start = (bf16[40,4096]{1,0:T(8,128)(2,1)S(1)}, bf16[40,4096]{1,0:T(8,128)(2,1)}, u32[]{:S(2)}) copy-start(bf16[40,4096]{1,0:T(8,128)(2,1)} %param.9) | copy-start | bytes 983044
  7.2 124.1 %all-gather.3.cloned.1.call-start = ((), (), s32[]{:S(2)}) async-start(), calls=%async_computation.4 | async-start | bytes 7864320 | tf_op jit(solution)/shard_map/all_gather | solution.py:72
  7.9 160.9 %reduce-scatter.2.cloned.1.call-start = ((), (), s32[]{:S(2)}) async-start(), calls=%async_computation.5 | async-start | bytes 2457600 | tf_op jit(solution)/shard_map/reduce_scatter | solution.py:80
  10.6 2.4 copy-start.1
  10.6 2.4 copy-start.2
  135.8 0.7 copy-start.4
  139.4 73.2 %all-to-all-start.2 = ((bf16[64,2,1536]{2,1,0:T(2,128)(2,1)}), bf16[64,2,1536]{2,1,0:T(2,128)(2,1)S(1)}, u32[]{:S(2)}, u32[]{:S(2)}) async-start(bf16[64,2,1536]{2,1,0:T(2,128)(2,1)} %reshape.148), calls=%async_computation.3 | async-start | bytes 786432 | tf_op jit(solution)/shard_map/all_to_all | solution.py:82
  147.8 57.7 %slice-start = ((bf16[1,768,512]{2,1,0:T(8,128)(2,1)}), bf16[1,640,512]{2,1,0:T(8,128)(2,1)S(1)}, s32[]{:S(2)}) async-start(bf16[1,768,512]{2,1,0:T(8,128)(2,1)} %param.14), calls=%async_computation.6 | async-start | bytes 1310720 | tf_op jit(solution)/shard_map/slice | solution.py:51
  211.2 42.2 %copy-start.3 = (f32[40,8]{0,1:T(8,128)S(1)}, f32[40,8]{0,1:T(8,128)}, u32[]{:S(2)}) copy-start(f32[40,8]{0,1:T(8,128)} %param.11) | copy-start | bytes 3844
  212.5 75.6 %all-to-all-start.1 = ((bf16[64,2,2560]{2,1,0:T(2,128)(2,1)}), bf16[64,2,2560]{2,1,0:T(2,128)(2,1)S(1)}, u32[]{:S(2)}, u32[]{:S(2)}) async-start(bf16[64,2,2560]{2,1,0:T(2,128)(2,1)} %reshape.146), calls=%async_computation.2 | async-start | bytes 1310720 | tf_op jit(solution)/shard_map/all_to_all | solution.py:90
Sparse Core Ops, SparseCore 0:
  10.1 78.4 all-gather.2
  136.0 32.8 reduce-scatter.1

commit v5 on v4

--- a/solution.py
+++ b/solution.py
@@ -80,7 +80,7 @@
     projected = lax.psum_scatter(partial, "y", scatter_dimension=0, tiled=False)
     hidden = (jax.nn.silu(projected[:hidden_count]) * projected[hidden_count:]).astype(jnp.bfloat16)
     back = lax.all_to_all(jnp.take(spread, partner, axis=0), "expert", split_axis=0, concat_axis=0, tiled=True)
-    every_hidden = lax.all_gather(lax.all_gather(hidden, "y", axis=0, tiled=False), "zh", axis=0, tiled=False)
+    every_hidden = lax.all_gather(lax.all_gather(hidden, "zh", axis=0, tiled=False), "y", axis=1, tiled=False)
     every_hidden = every_hidden.reshape(-1, hidden.shape[1])
     down_rows = down_new.reshape(-1, part_width)
     summed = lax.dot_general(

time: 302 us -> 275 us (0.911)
  starting transfers between devices: 49.4 us -> 32.4 us
  blocking collectives: 132 us -> 122 us
    all_to_all x1, starting transfers between devices: 40.9 us -> 23.9 us  [shards(): lax.all_to_all(results, 'expert', split_axis=0, concat_axis=0, tiled=True)]
    all_gather x2, blocking collectives: 35.5 us -> 26.1 us  [the longest x1 14.2 us: shards(): lax.all_gather(hidden, 'zh', axis=0, tiled=False)]
  transfers between devices with their start and end apart: 4 -> 4, of which waited for: 2 -> 2; matrix products, arithmetic and copies ran while one was open for 14% -> 15% of each run, Pallas kernels for 0% -> 0%
where the time goes in v5:
time: 275 us
  blocking collectives  122 us (44%)
  waiting for transfers between devices  53.3 us (19%)
  starting transfers between devices  32.4 us (12%)
  local copies, waits for them, and re-layouts  28.4 us (10%)
  other arithmetic  17.4 us (6%)
  between operations  14.3 us (5%)
  matrix products  6.77 us (2%)
    all_to_all x1, blocking collectives, shards(): lax.all_to_all(outgoing, 'expert', split_axis=0, concat_axis=0, tiled=True)  96.1 us
    all_to_all x1, waiting for transfers between devices, shards(): lax.all_to_all(results, 'expert', split_axis=0, concat_axis=0, tiled=True)  31.5 us
    all_to_all x1, starting transfers between devices, shards(): lax.all_to_all(results, 'expert', split_axis=0, concat_axis=0, tiled=True)  23.9 us
    reduce_scatter x1, waiting for transfers between devices, shards(): projected = lax.psum_scatter(partial, 'y', scatter_dimension=0, tiled=False)  21 us
    unnamed x20, local copies, waits for them, and re-layouts  16.4 us
    all_gather x1, blocking collectives, shards(): lax.all_gather(hidden, 'zh', axis=0, tiled=False)  14.2 us
    all_gather x1, blocking collectives, shards(): lax.all_gather(lax.all_gather(hidden, 'zh', axis=0, tiled=False), 'y', ax...  11.8 us
    all_to_all x2, other arithmetic, shards(): lax.all_to_all(results, 'expert', split_axis=0, concat_axis=0, tiled=True)  8.5 us
  transfers between devices with their start and end apart: 4, of which 2 were waited for; matrix products, arithmetic and copies ran while one was open for 15% of the time, Pallas kernels for 0%

profile of v5, /device:TPU:1, one launch (start us, length us, event | category | flops | bytes accessed | tf_op | source)
XLA Modules:
  0.0 274.7 jit_solution(16738527184922077938)
XLA Ops:
  7.2 0.7 all-gather.3.cloned.1.call-update
  8.0 0.8 copy.35
  8.7 0.1 eq.37
  8.9 0.9 reduce-window.6
  9.8 0.2 slice_reduce_fusion
  10.0 0.1 bitcast_bitcast_fusion
  10.3 0.3 convert_reduce_fusion
  10.6 0.5 convolution_convert_fusion
  11.2 1.9 reshape.109
  13.1 1.2 fusion.6
  14.3 0.7 reshape.110
  15.0 0.7 reshape.111
  15.7 0.7 reshape.112
  16.4 1.1 maximum_bitcast_fusion
  17.6 0.5 broadcast.70
  18.1 2.6 reduce.4
  20.7 5.1 %reshape.144 = bf16[64,2,6656]{2,1,0:T(2,128)(2,1)} reshape(bf16[64,13312]{1,0:T(8,128)(2,1)} %reduce.4) | data formatting | bytes 3407872
  25.8 96.1 %all_to_all.31 = bf16[64,2,6656]{2,1,0:T(2,128)(2,1)S(1)} all-to-all(bf16[64,2,6656]{2,1,0:T(2,128)(2,1)} %reshape.144), channel_id=1, replica_groups=mesh['expert'=64,'zh'=2,'y'=4] {'expert'}, dimensions={0} | all-to-all | bytes 3407872 | tf_op jit(solution)/shard_map/all_to_all | solution.py:74
  121.9 3.9 %reshape.145 = bf16[64,1,13312]{2,1,0:T(2,128)(2,1)} reshape(bf16[64,2,6656]{2,1,0:T(2,128)(2,1)S(1)} %all_to_all.31) | data formatting | bytes 3407872
  125.8 2.5 copy.51
  128.4 2.9 %reshape.138 = bf16[640,1024,1]{1,0,2:T(8,128)(2,1)} reshape(bf16[64,10240]{1,0:T(8,128)(2,1)S(1)} %slice.54) | data formatting | bytes 2621440 | tf_op jit(solution)/shard_map/reshape | solution.py:76
  131.3 4.5 %fusion = f32[4,192,640]{2,1,0:T(8,128)} fusion(bf16[640,1024,1]{1,0,2:T(8,128)(2,1)} %reshape.138, bf16[4,192,4096]{2,1,0:T(8,128)(2,1)} %all-gather.3.cloned.1.call-done, s32[]{:T(128)S(6)} %select_n.25), kind=kOutput, calls=%fused_computation.4 | convolution fusion | flops 1006632960 | bytes 4849668 | tf_op jit(solution)/shard_map/dot_general | solution.py:77
  135.8 0.6 copy-done.4
  136.5 0.8 gather_fusion
  137.3 0.1 bitcast_select_fusion
  137.4 0.9 reduce.6
  138.3 1.0 reshape.148
  139.4 8.4 %all-to-all-start.2 = ((bf16[64,2,1536]{2,1,0:T(2,128)(2,1)}), bf16[64,2,1536]{2,1,0:T(2,128)(2,1)S(1)}, u32[]{:S(2)}, u32[]{:S(2)}) async-start(bf16[64,2,1536]{2,1,0:T(2,128)(2,1)} %reshape.148), calls=%async_computation.3 | async-start | bytes 786432 | tf_op jit(solution)/shard_map/all_to_all | solution.py:82
  147.8 21.0 %reduce-scatter.2.cloned.1.call-done = f32[1,192,640]{2,1,0:T(8,128)} async-done(((f32[4,192,640]{2,1,0:T(8,128)}), f32[1,192,640]{2,1,0:T(8,128)}) %reduce-scatter.2.cloned.1.call-update) | async-done | bytes 491536 | tf_op jit(solution)/shard_map/reduce_scatter | solution.py:80
  168.8 1.1 fusion.9
  170.0 14.2 %all_gather.14 = bf16[2,96,640]{2,1,0:T(8,128)(2,1)S(1)} all-gather(bf16[1,96,640]{2,1,0:T(8,128)(2,1)S(1)} %fusion.9), channel_id=1, replica_groups=mesh['expert'=64,'zh'=2,'y'=4] {'zh'}, dimensions={0}, use_global_device_ids=true | all-gather | bytes 368640 | tf_op jit(solution)/shard_map/all_gather | solution.py:83
  184.2 11.8 %all-gather = bf16[2,384,640]{2,1,0:T(8,128)(2,1)S(1)} all-gather(bf16[2,96,640]{2,1,0:T(8,128)(2,1)S(1)} %all_gather.14), channel_id=2, replica_groups=mesh['expert'=64,'zh'=2,'y'=4] {'y'}, dimensions={1}, use_global_device_ids=true | all-gather | bytes 1228800 | tf_op jit(solution)/shard_map/all_gather | solution.py:83
  196.1 0.7 convolution_convert_fusion.1
  196.8 0.4 all_to_all.27
  197.2 4.6 %reduce.5 = bf16[64,5120]{1,0:T(8,128)(2,1)S(1)} reduce(bf16[64,1,5120]{2,1,0:T(2,128)(2,1)S(1)} %all_to_all.27, bf16[]{:T(256)} %broadcast.70), dimensions={1}, to_apply=%all_to_all.27.reduce_sub_computation | reduce | bytes 1310722 | tf_op jit(solution)/shard_map/all_to_all | solution.py:90
  201.7 1.3 reshape.146
  203.1 23.9 %all-to-all-start.1 = ((bf16[64,2,2560]{2,1,0:T(2,128)(2,1)}), bf16[64,2,2560]{2,1,0:T(2,128)(2,1)S(1)}, u32[]{:S(2)}, u32[]{:S(2)}) async-start(bf16[64,2,2560]{2,1,0:T(2,128)(2,1)} %reshape.146), calls=%async_computation.2 | async-start | bytes 1310720 | tf_op jit(solution)/shard_map/all_to_all | solution.py:90
  227.0 0.3 select_reduce_fusion
  227.4 0.3 reshape.149
  227.7 0.1 copy.52
  227.9 0.7 reshape.124
  228.6 0.7 reshape.126
  229.4 0.7 reshape.117
  230.1 31.5 %all-to-all-done.1 = bf16[64,2,2560]{2,1,0:T(2,128)(2,1)S(1)} async-done(((bf16[64,2,2560]{2,1,0:T(2,128)(2,1)}), bf16[64,2,2560]{2,1,0:T(2,128)(2,1)S(1)}, u32[]{:S(2)}, u32[]{:S(2)}) %all-to-all-start.1) | async-done | bytes 655392 | tf_op jit(solution)/shard_map/all_to_all | solution.py:90
  261.6 0.5 reshape.147
  262.1 3.9 %reduce.2 = bf16[64,5120]{1,0:T(8,128)(2,1)S(1)} reduce(bf16[64,1,5120]{2,1,0:T(2,128)(2,1)S(1)} %reshape.147, bf16[]{:T(256)} %constant.70), dimensions={1}, to_apply=%all_to_all.24.reduce_sub_computation | reduce | bytes 1310722 | tf_op jit(solution)/shard_map/all_to_all | solution.py:90
  266.1 0.8 reshape.116
  266.8 1.0 convolution_convert_fusion.2
  (29 shorter events, 0.6 us)
Async XLA Ops:
  7.2 3.4 %copy-start = (bf16[40,4096]{1,0:T(8,128)(2,1)S(1)}, bf16[40,4096]{1,0:T(8,128)(2,1)}, u32[]{:S(2)}) copy-start(bf16[40,4096]{1,0:T(8,128)(2,1)} %param.9) | copy-start | bytes 983044
  7.2 124.1 %all-gather.3.cloned.1.call-start = ((), (), s32[]{:S(2)}) async-start(), calls=%async_computation.4 | async-start | bytes 7864320 | tf_op jit(solution)/shard_map/all_gather | solution.py:72
  7.9 160.9 %reduce-scatter.2.cloned.1.call-start = ((), (), s32[]{:S(2)}) async-start(), calls=%async_computation.5 | async-start | bytes 2457600 | tf_op jit(solution)/shard_map/reduce_scatter | solution.py:80
  10.6 2.4 copy-start.1
  10.6 2.4 copy-start.2
  135.8 0.7 copy-start.4
  139.4 63.7 %all-to-all-start.2 = ((bf16[64,2,1536]{2,1,0:T(2,128)(2,1)}), bf16[64,2,1536]{2,1,0:T(2,128)(2,1)S(1)}, u32[]{:S(2)}, u32[]{:S(2)}) async-start(bf16[64,2,1536]{2,1,0:T(2,128)(2,1)} %reshape.148), calls=%async_computation.3 | async-start | bytes 786432 | tf_op jit(solution)/shard_map/all_to_all | solution.py:82
  147.8 48.3 %slice-start = ((bf16[1,768,512]{2,1,0:T(8,128)(2,1)}), bf16[1,640,512]{2,1,0:T(8,128)(2,1)S(1)}, s32[]{:S(2)}) async-start(bf16[1,768,512]{2,1,0:T(8,128)(2,1)} %param.14), calls=%async_computation.6 | async-start | bytes 1310720 | tf_op jit(solution)/shard_map/slice | solution.py:51
  201.7 25.2 %copy-start.3 = (f32[40,8]{0,1:T(8,128)S(1)}, f32[40,8]{0,1:T(8,128)}, u32[]{:S(2)}) copy-start(f32[40,8]{0,1:T(8,128)} %param.11) | copy-start | bytes 3844
  203.1 58.5 %all-to-all-start.1 = ((bf16[64,2,2560]{2,1,0:T(2,128)(2,1)}), bf16[64,2,2560]{2,1,0:T(2,128)(2,1)S(1)}, u32[]{:S(2)}, u32[]{:S(2)}) async-start(bf16[64,2,2560]{2,1,0:T(2,128)(2,1)} %reshape.146), calls=%async_computation.2 | async-start | bytes 1310720 | tf_op jit(solution)/shard_map/all_to_all | solution.py:90
Sparse Core Ops, SparseCore 0:
  10.1 78.4 all-gather.2
  136.0 32.8 reduce-scatter.1
